TPU v7x, 32 devices: a whole 2x2x4 slice. The times are simulated.
32 devices in a mesh: dp: 8 (over z, core), rot: 4 (over y, x).
Axes of the slice: x: 2, y: 2, z: 4, core: 2. Of those that a mesh axis runs over, the one named last changes fastest.
Arguments:
- vectors: bfloat16 [2048, 4096], P('dp', 'rot'), may hold values from -100 to 100
- rotation: bfloat16 [4096, 4096], P('rot'), may hold values from -0.125 to 0.125
- codes: int32 [2048, 256], P('dp', 'rot'), may hold values from 0 to 255
Outputs:
- codebook: float32 [4096, 256], P('rot')
- new_rotation: bfloat16 [4096, 4096], P('rot', 'dp')
All inputs are finite; a program needn't handle non-finite values.
Results may differ from a plain program's by a relative error of at most 0.007.
Values may be sent and summed in bfloat16 or wider, within the bound.
No kernel may reach another device: no remote copies, remote signals or barrier semaphores. Data moves between devices by JAX's collectives and lax.ppermute only.
A program may use at most 64 MiB of HBM per device.

v0:
```python
import math
import jax
import jax.numpy as jnp
from jax import lax
from jax.sharding import PartitionSpec as P

K = 256
ITERS = 2


def body(vectors, rotation, codes):
    row_count, block_dims = vectors.shape
    width = rotation.shape[1]
    local_spaces = codes.shape[1]
    sub_dims = block_dims // local_spaces
    tile_cols = width // lax.axis_size("dp")
    tile_spaces = tile_cols // sub_dims
    dp_index = lax.axis_index("dp")
    code_ids = jnp.arange(K, dtype=jnp.int32)
    dp_size = lax.axis_size("dp")
    row_codes = lax.all_gather(codes, "rot", axis=1, tiled=True)

    def block_codes(block):
        return lax.dynamic_slice_in_dim(row_codes, block * tile_spaces, tile_spaces, 1).astype(
            jnp.bfloat16
        )

    if dp_size % 2:
        parts = [jnp.concatenate([vectors, block_codes(dp_index)], axis=1)]
        for shift in range(1, dp_size):
            pairs = [(i, (i + shift) % dp_size) for i in range(dp_size)]
            target = (dp_index + shift) % dp_size
            parts.append(
                lax.ppermute(jnp.concatenate([vectors, block_codes(target)], axis=1), "dp", pairs)
            )
        joined = jnp.concatenate(parts, axis=0)
    else:

        def pair_part(block):
            return jnp.concatenate([vectors, block_codes(block), block_codes(block ^ 1)], axis=1)

        parts = [pair_part(dp_index)]
        for shift in range(2, dp_size, 2):
            pairs = [(i, (i + shift) % dp_size) for i in range(dp_size)]
            parts.append(lax.ppermute(pair_part((dp_index + shift) % dp_size), "dp", pairs))
        group = jnp.concatenate(parts, axis=0)
        mine = group[:, : block_dims + tile_spaces]
        for_mate = jnp.concatenate(
            [group[:, :block_dims], group[:, block_dims + tile_spaces :]], axis=1
        )
        mates = [(i, i ^ 1) for i in range(dp_size)]
        joined = jnp.concatenate([mine, lax.ppermute(for_mate, "dp", mates)], axis=0)
    all_vectors = joined[:, :block_dims]
    tile_codes = joined[:, block_dims:].astype(jnp.int32)
    rotated_t = lax.psum_scatter(
        lax.dot_general(
            rotation, vectors, (((0,), (1,)), ((), ())), preferred_element_type=jnp.float32
        ),
        "rot",
        scatter_dimension=0,
        tiled=True,
    ).astype(jnp.bfloat16)
    code_indicator = (codes.T[:, :, None] == code_ids[None, None, :]).astype(jnp.bfloat16)
    grouped_vectors = rotated_t.reshape(local_spaces, sub_dims, row_count)
    shard_code_sums = jnp.einsum(
        "vzo,voc->vzc", grouped_vectors, code_indicator, preferred_element_type=jnp.float32
    )
    local_counts = jnp.sum(code_indicator, axis=1, dtype=jnp.float32)
    total_sums, total_counts = lax.psum((shard_code_sums, local_counts), "dp")
    book = total_sums / jnp.maximum(total_counts, 1.0)[:, None, :]
    codebook = book.reshape(block_dims, K)
    blocks_per_rot = local_spaces // tile_spaces
    offered = lax.dynamic_slice_in_dim(
        book.astype(jnp.bfloat16), dp_index % blocks_per_rot * tile_spaces, tile_spaces, 0
    )
    tile_book = lax.all_gather(offered, "rot", axis=0)[dp_index // blocks_per_rot]
    tile_book, all_vectors, tile_codes = lax.optimization_barrier(
        (tile_book, all_vectors, tile_codes)
    )
    tile_indicator = (tile_codes.T[:, :, None] == code_ids[None, None, :]).astype(jnp.bfloat16)
    rebuilt_t = jnp.einsum(
        "lyg,lxg->lyx", tile_book, tile_indicator, preferred_element_type=jnp.float32
    )
    rebuilt_t = rebuilt_t.astype(jnp.bfloat16).reshape(tile_cols, all_vectors.shape[0])
    cross_tile = lax.dot_general(
        all_vectors, rebuilt_t, (((0,), (1,)), ((), ())), preferred_element_type=jnp.float32
    ).astype(jnp.bfloat16)

    def apply_gram(rows_b, gram_b):
        return jnp.dot(
            rows_b,
            lax.all_gather(gram_b, "rot", axis=0, tiled=True),
            preferred_element_type=jnp.float32,
        )

    columns = cross_tile
    new_tile = None
    for iteration in range(ITERS):
        rows_b = lax.all_gather(columns, "dp", axis=1, tiled=True)
        partial = lax.dot_general(
            rows_b, columns, (((0,), (0,)), ((), ())), preferred_element_type=jnp.float32
        ).astype(jnp.bfloat16)
        if iteration == 0:
            gram_part = lax.psum_scatter(partial, "rot", scatter_dimension=0, tiled=True)
        else:
            gram_part = lax.psum(partial, "rot")
        if iteration == 0:
            gram_f = gram_part.astype(jnp.float32)
            total = lax.psum(jnp.sum(gram_f * gram_f), ("dp", "rot"))
            factor = 1.7 / jnp.sqrt(jnp.sqrt(total))
            product = apply_gram(rows_b, gram_part)
            new_tile = factor * (
                1.5 * columns.astype(jnp.float32) - 0.5 * (factor * factor) * product
            )
        else:
            product = jnp.dot(rows_b, gram_part, preferred_element_type=jnp.float32)
            new_tile = 1.5 * columns.astype(jnp.float32) - 0.5 * product
        columns = new_tile.astype(jnp.bfloat16)
    new_rotation = (math.sqrt(width) * new_tile).astype(jnp.bfloat16)
    return (codebook, new_rotation)


def solution(mesh):
    return jax.shard_map(
        body,
        mesh=mesh,
        in_specs=(P("dp", "rot"), P("rot", None), P("dp", "rot")),
        out_specs=(P("rot", None), P("rot", "dp")),
        check_vma=False,
    )
```

profile of v0, /device:TPU:0, one launch (start us, length us, event | category | flops | bytes accessed | tf_op | source)
XLA Modules:
  0.0 616.0 jit_solution(11668680264245755234)
XLA Ops:
  7.2 0.0 reduce-scatter.3.cloned.1.call-start
  7.2 7.8 %fusion.19 = f32[4096,256]{1,0:T(8,128)} fusion(bf16[1024,4096]{1,0:T(8,128)(2,1)} %param.4, bf16[256,1024]{1,0:T(8,128)(2,1)} %param.3), kind=kOutput, calls=%fused_computation.48 | convolution fusion | flops 2147483648 | bytes 13107200 | tf_op jit(solution)/shard_map/dot_general | solution.py:56
  15.1 0.0 reduce-scatter.3.cloned.1.call-update
  15.1 0.0 all-reduce.6.cloned.1.call-start
  15.2 0.9 copy-done.6
  16.1 0.2 copy.14
  16.3 0.0 copy-done.7
  16.4 11.0 %all_gather.20 = s32[256,256]{0,1:T(8,128)S(1)} all-gather(s32[256,64]{0,1:T(8,128)S(1)} %copy-done.7), channel_id=1, replica_groups=mesh['dp'=8,'rot'=4] {'rot'}, dimensions={1}, use_global_device_ids=true | all-gather | bytes 327680 | tf_op jit(solution)/shard_map/all_gather | solution.py:21
  27.4 0.1 pad_maximum_fusion.1
  27.5 1.8 collective-permute-start
  29.3 3.0 collective-permute-start.1
  32.3 1.2 collective-permute-start.2
  33.4 3.4 convert_reduce_fusion
  36.9 8.4 %collective-permute-done = bf16[256,1088]{0,1:T(8,128)(2,1)S(1)} collective-permute-done((bf16[256,1088]{0,1:T(8,128)(2,1)S(1)}, bf16[256,1088]{0,1:T(8,128)(2,1)S(1)}, u32[]{:S(2)}, u32[]{:S(2)}) %collective-permute-start) | collective-permute-done | bytes 557088 | tf_op jit(solution)/shard_map/ppermute | solution.py:45
  45.3 19.9 %collective-permute-done.1 = bf16[256,1088]{0,1:T(8,128)(2,1)S(1)} collective-permute-done((bf16[256,1088]{0,1:T(8,128)(2,1)S(1)}, bf16[256,1088]{0,1:T(8,128)(2,1)S(1)}, u32[]{:S(2)}, u32[]{:S(2)}) %collective-permute-start.1) | collective-permute-done | bytes 557088 | tf_op jit(solution)/shard_map/ppermute | solution.py:45
  65.2 0.0 collective-permute-done.2
  65.2 0.8 copy-done.1
  66.0 0.2 copy-done.2
  66.2 2.4 pad_maximum_fusion
  68.7 1.5 slice.21
  70.2 1.0 reduce-scatter.3.cloned.1.call-done
  71.2 1.3 convert_element_type.67
  72.5 5.1 fusion.3
  77.6 0.0 all-reduce.6.cloned.1.call-update
  77.6 0.0 all-gather.12.cloned.1.call-start
  77.7 4.2 fusion.17
  81.9 0.0 collective-permute-start.3
  81.9 64.6 %all-reduce.6.cloned.1.call-done = (f32[64,16,256]{2,1,0:T(8,128)}, f32[64,256]{1,0:T(8,128)}) async-done(((f32[64,16,256]{2,1,0:T(8,128)}, f32[64,256]{1,0:T(8,128)}), (f32[64,16,256]{2,1,0:T(8,128)}, f32[64,256]{1,0:T(8,128)})) %all-reduce.6.cloned.1.call-update) | async-done | bytes 1114128 | tf_op jit(solution)/shard_map/psum | solution.py:69
  146.5 0.8 broadcast_maximum_fusion
  147.3 1.3 broadcast_divide_fusion
  148.7 0.0 copy-start.3
  148.7 0.8 dynamic-slice_convert_fusion
  149.5 0.0 all-gather.12.cloned.1.call-update
  149.5 0.0 all-gather.6.cloned.1.call-start
  149.6 0.2 slice.20
  149.8 0.0 collective-permute-done.3
  149.8 0.9 fusion.18
  150.7 0.0 copy-done.3
  150.7 3.4 fusion.10
  154.1 21.1 %all-gather.12.cloned.1.call-done = bf16[128,16,256]{2,1,0:T(8,128)(2,1)} async-done(((bf16[32,16,256]{2,1,0:T(8,128)(2,1)}), bf16[128,16,256]{2,1,0:T(8,128)(2,1)}) %all-gather.12.cloned.1.call-update) | async-done | bytes 1048592 | tf_op jit(solution)/shard_map/all_gather | solution.py:76
  175.2 1.0 dynamic-slice_bitcast_fusion
  176.2 0.0 copy-start
  176.2 16.1 %fusion.11 = bf16[32,16,2048]{2,1,0:T(8,128)(2,1)S(1)} fusion(bf16[32,16,256]{2,1,0:T(8,128)(2,1)S(1)} %dynamic-slice_bitcast_fusion, s32[32,2048]{1,0:T(8,128)S(1)} %bitcast.25), kind=kOutput, calls=%fused_computation.19 | convolution fusion | flops 554696704 | bytes 2621440 | tf_op jit(solution)/shard_map/lyg,lxg->lyx/dot_general | solution.py:81
  192.3 3.3 convolution_convert_fusion.2
  195.6 0.0 all-gather.6.cloned.1.call-update
  195.6 0.2 reduce-scatter.5.cloned.1.call-start
  195.9 82.0 %all-gather.6.cloned.1.call-done = bf16[1024,4096]{1,0:T(8,128)(2,1)} async-done(((bf16[1024,512]{1,0:T(8,128)(2,1)}), bf16[1024,4096]{1,0:T(8,128)(2,1)}) %all-gather.6.cloned.1.call-update) | async-done | bytes 8388624 | tf_op jit(solution)/shard_map/all_gather | solution.py:99
  277.8 10.2 %convolution_convert_fusion.1 = bf16[4096,512]{1,0:T(8,128)(2,1)} fusion(bf16[1024,4096]{1,0:T(8,128)(2,1)} %all-gather.6.cloned.1.call-done, bf16[1024,512]{1,0:T(8,128)(2,1)} %convolution_convert_fusion.2), kind=kOutput, calls=%fused_computation.9 | convolution fusion | flops 4297064448 | bytes 13631488 | tf_op jit(solution)/shard_map/dot_general | solution.py:100
  288.0 0.0 reduce-scatter.5.cloned.1.call-update
  288.0 0.0 all-gather.8.cloned.1.call-start
  288.0 51.2 %reduce-scatter.5.cloned.1.call-done = bf16[1024,512]{1,0:T(8,128)(2,1)} async-done(((bf16[4096,512]{1,0:T(8,128)(2,1)}), bf16[1024,512]{1,0:T(8,128)(2,1)}) %reduce-scatter.5.cloned.1.call-update) | async-done | bytes 1048592 | tf_op jit(solution)/shard_map/reduce_scatter | solution.py:104
  339.2 0.0 all-gather.8.cloned.1.call-update
  339.3 0.0 all-gather.10.cloned.1.call-start
  339.3 2.4 multiply_reduce_fusion
  341.7 40.3 %psum.30 = f32[]{:T(128)} all-reduce(f32[]{:T(128)} %multiply_reduce_fusion), channel_id=1, replica_groups=mesh['dp'=8,'rot'=4] {'dp','rot'}, use_global_device_ids=true, to_apply=%region_6.7 | all-reduce | flops 1 | bytes 8 | tf_op jit(solution)/shard_map/psum | solution.py:109
  382.7 11.6 %all-gather.8.cloned.1.call-done = bf16[4096,512]{1,0:T(8,128)(2,1)} async-done(((bf16[1024,512]{1,0:T(8,128)(2,1)}), bf16[4096,512]{1,0:T(8,128)(2,1)}) %all-gather.8.cloned.1.call-update) | async-done | bytes 4194320 | tf_op jit(solution)/shard_map/all_gather | solution.py:92
  394.4 10.1 %multiply_convert_fusion.1 = bf16[1024,512]{1,0:T(8,128)(2,1)} fusion(bf16[1024,512]{1,0:T(8,128)(2,1)S(1)} %copy-done.4, bf16[1024,4096]{1,0:T(8,128)(2,1)} %all-gather.6.cloned.1.call-done, bf16[4096,512]{1,0:T(8,128)(2,1)} %all-gather.8.cloned.1.call-done, f32[]{:T(128)S(6)} %mul.79, f32[]{:T(128)S(6)} %div.24), kind=kOutput, calls=%fused_computation.28 | convolution fusion | flops 4298113024 | bytes 14680072 | tf_op jit(solution)/shard_map/dot_general | solution.py:90
  404.5 0.0 all-gather.10.cloned.1.call-update
  404.5 0.3 all-reduce.4.cloned.1.call-start
  404.7 81.9 %all-gather.10.cloned.1.call-done = bf16[1024,4096]{1,0:T(8,128)(2,1)} async-done(((bf16[1024,512]{1,0:T(8,128)(2,1)}), bf16[1024,4096]{1,0:T(8,128)(2,1)}) %all-gather.10.cloned.1.call-update) | async-done | bytes 8388624 | tf_op jit(solution)/shard_map/all_gather | solution.py:99
  486.7 10.1 %convolution_convert_fusion = bf16[4096,512]{1,0:T(8,128)(2,1)} fusion(bf16[1024,4096]{1,0:T(8,128)(2,1)} %all-gather.10.cloned.1.call-done, bf16[1024,512]{1,0:T(8,128)(2,1)} %multiply_convert_fusion.1), kind=kOutput, calls=%fused_computation.8 | convolution fusion | flops 4297064448 | bytes 13631488 | tf_op jit(solution)/shard_map/dot_general | solution.py:100
  496.8 0.0 all-reduce.4.cloned.1.call-update
  496.8 102.3 %all-reduce.4.cloned.1.call-done = bf16[4096,512]{1,0:T(8,128)(2,1)} async-done(((bf16[4096,512]{1,0:T(8,128)(2,1)}), bf16[4096,512]{1,0:T(8,128)(2,1)}) %all-reduce.4.cloned.1.call-update) | async-done | bytes 4194320 | tf_op jit(solution)/shard_map/psum | solution.py:106
  599.1 10.1 %multiply_convert_fusion = bf16[1024,512]{1,0:T(8,128)(2,1)} fusion(bf16[1024,512]{1,0:T(8,128)(2,1)S(1)} %copy-done.5, bf16[1024,4096]{1,0:T(8,128)(2,1)} %all-gather.10.cloned.1.call-done, bf16[4096,512]{1,0:T(8,128)(2,1)} %all-reduce.4.cloned.1.call-done), kind=kOutput, calls=%fused_computation.27 | convolution fusion | flops 4298113024 | bytes 14680064 | tf_op jit(solution)/shard_map/dot_general | solution.py:116
  (10 shorter events, 0.0 us)
Async XLA Ops:
  7.2 64.0 %reduce-scatter.3.cloned.1.call-start = ((), (), s32[]{:S(2)}) async-start(), calls=%async_computation.2 | async-start | bytes 5242880 | tf_op jit(solution)/shard_map/reduce_scatter | solution.py:55
  15.1 1.0 copy-start.6
  15.1 1.3 copy-start.7
  15.1 131.4 %all-reduce.6.cloned.1.call-start = ((), (), s32[]{:S(2)}) async-start(), calls=%async_computation.9 | async-start | bytes 2228224 | tf_op jit(solution)/shard_map/psum | solution.py:69
  27.5 17.8 %collective-permute-start = (bf16[256,1088]{0,1:T(8,128)(2,1)S(1)}, bf16[256,1088]{0,1:T(8,128)(2,1)S(1)}, u32[]{:S(2)}, u32[]{:S(2)}) collective-permute-start(bf16[256,1088]{0,1:T(8,128)(2,1)S(1)} %get-tuple-element.10), channel_id=1, source_target_pairs={{0,8},{4,12},{8,16},{12,20},{16,24},{20,28},{24,0},{28,4},{1,9},{5... | collective-permute-start | bytes 1671176 | tf_op jit(solution)/shard_map/ppermute | solution.py:45
  29.3 35.9 %collective-permute-start.1 = (bf16[256,1088]{0,1:T(8,128)(2,1)S(1)}, bf16[256,1088]{0,1:T(8,128)(2,1)S(1)}, u32[]{:S(2)}, u32[]{:S(2)}) collective-permute-start(bf16[256,1088]{0,1:T(8,128)(2,1)S(1)} %get-tuple-element.11), channel_id=1, source_target_pairs={{0,16},{4,20},{8,24},{12,28},{16,0},{20,4},{24,8},{28,12},{1,17},{... | collective-permute-start | bytes 1671176 | tf_op jit(solution)/shard_map/ppermute | solution.py:45
  32.3 33.0 %collective-permute-start.2 = (bf16[256,1088]{0,1:T(8,128)(2,1)S(1)}, bf16[256,1088]{0,1:T(8,128)(2,1)S(1)}, u32[]{:S(2)}, u32[]{:S(2)}) collective-permute-start(bf16[256,1088]{0,1:T(8,128)(2,1)S(1)} %get-tuple-element.12), channel_id=1, source_target_pairs={{0,24},{4,28},{8,0},{12,4},{16,8},{20,12},{24,16},{28,20},{1,25},{... | collective-permute-start | bytes 1671176 | tf_op jit(solution)/shard_map/ppermute | solution.py:45
  65.2 0.8 copy-start.1
  65.2 1.0 copy-start.2
  77.6 97.6 %all-gather.12.cloned.1.call-start = ((), (), s32[]{:S(2)}) async-start(), calls=%async_computation.8 | async-start | bytes 1310720 | tf_op jit(solution)/shard_map/all_gather | solution.py:76
  81.9 67.9 %collective-permute-start.3 = (bf16[1024,1056]{0,1:T(8,128)(2,1)}, bf16[1024,1056]{0,1:T(8,128)(2,1)}, u32[]{:S(2)}, u32[]{:S(2)}) collective-permute-start(bf16[1024,1056]{0,1:T(8,128)(2,1)} %fusion.17), channel_id=1, source_target_pairs={{0,4},{4,0},{8,12},{12,8},{16,20},{20,16},{24,28},{28,24},{1,5},{5... | collective-permute-start | bytes 6488072 | tf_op jit(solution)/shard_map/ppermute | solution.py:52
  148.7 2.0 copy-start.3
  149.5 128.3 %all-gather.6.cloned.1.call-start = ((), (), s32[]{:S(2)}) async-start(), calls=%async_computation.3 | async-start | bytes 9437184 | tf_op jit(solution)/shard_map/all_gather | solution.py:99
  176.2 16.1 %copy-start = (bf16[2048,1024]{0,1:T(8,128)(2,1)S(1)}, bf16[2048,1024]{0,1:T(8,128)(2,1)}, u32[]{:S(2)}) copy-start(bf16[2048,1024]{0,1:T(8,128)(2,1)} %fusion.10) | copy-start | bytes 12582916
  195.6 143.6 %reduce-scatter.5.cloned.1.call-start = ((), (), s32[]{:S(2)}) async-start(), calls=%async_computation.4 | async-start | bytes 5242880 | tf_op jit(solution)/shard_map/reduce_scatter | solution.py:104
  288.0 106.4 %copy-start.4 = (bf16[1024,512]{1,0:T(8,128)(2,1)S(1)}, bf16[1024,512]{1,0:T(8,128)(2,1)}, u32[]{:S(2)}) copy-start(bf16[1024,512]{1,0:T(8,128)(2,1)} %convolution_convert_fusion.2) | copy-start | bytes 3145732
  288.0 106.4 %all-gather.8.cloned.1.call-start = ((), (), s32[]{:S(2)}) async-start(), calls=%async_computation.5 | async-start | bytes 5242880 | tf_op jit(solution)/shard_map/all_gather | solution.py:92
  339.3 147.4 %all-gather.10.cloned.1.call-start = ((), (), s32[]{:S(2)}) async-start(), calls=%async_computation.6 | async-start | bytes 9437184 | tf_op jit(solution)/shard_map/all_gather | solution.py:99
  404.5 194.6 %all-reduce.4.cloned.1.call-start = ((), (), s32[]{:S(2)}) async-start(), calls=%async_computation.7 | async-start | bytes 8388608 | tf_op jit(solution)/shard_map/psum | solution.py:106
  496.8 102.3 %copy-start.5 = (bf16[1024,512]{1,0:T(8,128)(2,1)S(1)}, bf16[1024,512]{1,0:T(8,128)(2,1)}, u32[]{:S(2)}) copy-start(bf16[1024,512]{1,0:T(8,128)(2,1)} %multiply_convert_fusion.1) | copy-start | bytes 3145732
Sparse Core Ops, SparseCore 0:
  15.2 55.9 reduce-scatter.2
  77.7 68.7 all-reduce.5
  149.7 25.4 all-gather.11
  195.7 82.0 all-gather.5
  288.1 51.0 reduce-scatter.4
  340.9 53.3 all-gather.7
  404.6 82.0 all-gather.9
  496.9 102.0 all-reduce.3
where the time goes:
time: 616 us
  waiting for transfers between devices  444 us (72%)
  matrix products  72.8 us (12%)
  blocking collectives  51.3 us (8%)
  other arithmetic  20.3 us (3%)
  between operations  15.1 us (2%)
  starting transfers between devices  6.66 us (1%)
    all_gather x2, waiting for transfers between devices, body(): rows_b = lax.all_gather(columns, 'dp', axis=1, tiled=True)  164 us
    psum x1, waiting for transfers between devices, body(): gram_part = lax.psum(partial, 'rot')  102 us
    psum x1, waiting for transfers between devices, body(): total_sums, total_counts = lax.psum((shard_code_sums, local_counts), 'dp')  64.6 us
    reduce_scatter x1, waiting for transfers between devices, body(): lax.psum_scatter(partial, 'rot', scatter_dimension=0, tiled=True)  51.2 us
    psum x1, blocking collectives, body(): total = lax.psum(jnp.sum(gram_f * gram_f), ('dp', 'rot'))  40.3 us
    ppermute x3, waiting for transfers between devices, body(): lax.ppermute(pair_part((dp_index + shift) % dp_size), 'dp', pairs)  28.4 us
    all_gather x1, waiting for transfers between devices, body(): lax.all_gather(offered, 'rot', axis=0)[dp_index // blocks_per_rot]  21.1 us
    dot_general x2, matrix products, body(): lax.dot_general(rows_b, columns, (((0,), (0,)), ((), ())), preferred_elem...  20.3 us
  transfers between devices with their start and end apart: 12, of which 10 were waited for; matrix products, arithmetic and copies ran while one was open for 4% of the time, Pallas kernels for 0%

commit v1 on v0

--- a/solution.py
+++ b/solution.py
@@ -103,7 +103,11 @@
         if iteration == 0:
             gram_part = lax.psum_scatter(partial, "rot", scatter_dimension=0, tiled=True)
         else:
-            gram_part = lax.psum(partial, "rot")
+
+            def assign_the_domain(xx):
+                return jnp.sum(lax.all_gather(xx, axis_name="rot"), axis=0)
+
+            gram_part = assign_the_domain(partial)
         if iteration == 0:
             gram_f = gram_part.astype(jnp.float32)
             total = lax.psum(jnp.sum(gram_f * gram_f), ("dp", "rot"))

time: 616 us -> 682 us (1.11)
  waiting for transfers between devices: 444 us -> 498 us
  other arithmetic: 20.3 us -> 32.1 us
    all_gather x0 -> x1, waiting for transfers between devices: none -> 156 us  [assign_the_domain(): return jnp.sum(lax.all_gather(xx, axis_name='rot'), axis=0)]
    psum x1 -> x0, waiting for transfers between devices: 102 us -> none  [body(): gram_part = lax.psum(partial, 'rot')]
    reduce_sum x0 -> x1, other arithmetic: none -> 11.8 us  [assign_the_domain(): return jnp.sum(lax.all_gather(xx, axis_name='rot'), axis=0)]
  transfers between devices with their start and end apart: 12 -> 12, of which waited for: 10 -> 10; matrix products, arithmetic and copies ran while one was open for 4% -> 3% of each run, Pallas kernels for 0% -> 0%
where the time goes in v1:
time: 682 us
  waiting for transfers between devices  498 us (73%)
  matrix products  72.9 us (11%)
  blocking collectives  51.4 us (8%)
  other arithmetic  32.1 us (5%)
  between operations  15.1 us (2%)
    all_gather x2, waiting for transfers between devices, body(): rows_b = lax.all_gather(columns, 'dp', axis=1, tiled=True)  164 us
    all_gather x1, waiting for transfers between devices, assign_the_domain(): return jnp.sum(lax.all_gather(xx, axis_name='rot'), axis=0)  156 us
    psum x1, waiting for transfers between devices, body(): total_sums, total_counts = lax.psum((shard_code_sums, local_counts), 'dp')  64.6 us
    reduce_scatter x1, waiting for transfers between devices, body(): lax.psum_scatter(partial, 'rot', scatter_dimension=0, tiled=True)  51.2 us
    psum x1, blocking collectives, body(): total = lax.psum(jnp.sum(gram_f * gram_f), ('dp', 'rot'))  40.4 us
    ppermute x3, waiting for transfers between devices, body(): lax.ppermute(pair_part((dp_index + shift) % dp_size), 'dp', pairs)  28.4 us
    all_gather x1, waiting for transfers between devices, body(): lax.all_gather(offered, 'rot', axis=0)[dp_index // blocks_per_rot]  21.1 us
    dot_general x2, matrix products, body(): lax.dot_general(rows_b, columns, (((0,), (0,)), ((), ())), preferred_elem...  20.3 us
  transfers between devices with their start and end apart: 12, of which 10 were waited for; matrix products, arithmetic and copies ran while one was open for 3% of the time, Pallas kernels for 0%

profile of v1, /device:TPU:0, one launch (start us, length us, event | category | flops | bytes accessed | tf_op | source)
XLA Modules:
  0.0 681.5 jit_solution(14553981289793590363)
XLA Ops:
  7.2 0.0 reduce-scatter.3.cloned.1.call-start
  7.2 7.8 %fusion.19 = f32[4096,256]{1,0:T(8,128)} fusion(bf16[1024,4096]{1,0:T(8,128)(2,1)} %param.4, bf16[256,1024]{1,0:T(8,128)(2,1)} %param.3), kind=kOutput, calls=%fused_computation.48 | convolution fusion | flops 2147483648 | bytes 13107200 | tf_op jit(solution)/shard_map/dot_general | solution.py:56
  15.1 0.0 reduce-scatter.3.cloned.1.call-update
  15.1 0.0 all-reduce.3.cloned.1.call-start
  15.2 0.9 copy-done.6
  16.1 0.2 copy.14
  16.3 0.0 copy-done.7
  16.4 11.0 %all_gather.26 = s32[256,256]{0,1:T(8,128)S(1)} all-gather(s32[256,64]{0,1:T(8,128)S(1)} %copy-done.7), channel_id=1, replica_groups=mesh['dp'=8,'rot'=4] {'rot'}, dimensions={1}, use_global_device_ids=true | all-gather | bytes 327680 | tf_op jit(solution)/shard_map/all_gather | solution.py:21
  27.4 0.1 pad_maximum_fusion.1
  27.5 1.8 collective-permute-start
  29.3 3.0 collective-permute-start.1
  32.3 1.2 collective-permute-start.2
  33.4 3.4 convert_reduce_fusion
  36.9 8.4 %collective-permute-done = bf16[256,1088]{0,1:T(8,128)(2,1)S(1)} collective-permute-done((bf16[256,1088]{0,1:T(8,128)(2,1)S(1)}, bf16[256,1088]{0,1:T(8,128)(2,1)S(1)}, u32[]{:S(2)}, u32[]{:S(2)}) %collective-permute-start) | collective-permute-done | bytes 557088 | tf_op jit(solution)/shard_map/ppermute | solution.py:45
  45.3 19.9 %collective-permute-done.1 = bf16[256,1088]{0,1:T(8,128)(2,1)S(1)} collective-permute-done((bf16[256,1088]{0,1:T(8,128)(2,1)S(1)}, bf16[256,1088]{0,1:T(8,128)(2,1)S(1)}, u32[]{:S(2)}, u32[]{:S(2)}) %collective-permute-start.1) | collective-permute-done | bytes 557088 | tf_op jit(solution)/shard_map/ppermute | solution.py:45
  65.2 0.0 collective-permute-done.2
  65.2 0.8 copy-done.1
  66.0 0.2 copy-done.2
  66.2 2.4 pad_maximum_fusion
  68.7 1.5 slice.21
  70.2 1.0 reduce-scatter.3.cloned.1.call-done
  71.2 1.3 convert_element_type.69
  72.5 5.1 fusion.3
  77.6 0.0 all-reduce.3.cloned.1.call-update
  77.6 0.0 all-gather.14.cloned.1.call-start
  77.7 4.2 fusion.17
  81.9 0.0 collective-permute-start.3
  81.9 64.6 %all-reduce.3.cloned.1.call-done = (f32[64,16,256]{2,1,0:T(8,128)}, f32[64,256]{1,0:T(8,128)}) async-done(((f32[64,16,256]{2,1,0:T(8,128)}, f32[64,256]{1,0:T(8,128)}), (f32[64,16,256]{2,1,0:T(8,128)}, f32[64,256]{1,0:T(8,128)})) %all-reduce.3.cloned.1.call-update) | async-done | bytes 1114128 | tf_op jit(solution)/shard_map/psum | solution.py:69
  146.5 0.8 broadcast_maximum_fusion
  147.3 1.3 broadcast_divide_fusion
  148.7 0.0 copy-start.3
  148.7 0.8 dynamic-slice_convert_fusion
  149.5 0.0 all-gather.14.cloned.1.call-update
  149.5 0.0 all-gather.8.cloned.1.call-start
  149.6 0.2 slice.20
  149.8 0.0 collective-permute-done.3
  149.8 0.9 fusion.18
  150.7 3.4 fusion.10
  154.1 21.1 %all-gather.14.cloned.1.call-done = bf16[128,16,256]{2,1,0:T(8,128)(2,1)} async-done(((bf16[32,16,256]{2,1,0:T(8,128)(2,1)}), bf16[128,16,256]{2,1,0:T(8,128)(2,1)}) %all-gather.14.cloned.1.call-update) | async-done | bytes 1048592 | tf_op jit(solution)/shard_map/all_gather | solution.py:76
  175.2 1.0 dynamic-slice_bitcast_fusion
  176.2 16.1 %fusion.11 = bf16[32,16,2048]{2,1,0:T(8,128)(2,1)S(1)} fusion(bf16[32,16,256]{2,1,0:T(8,128)(2,1)S(1)} %dynamic-slice_bitcast_fusion, s32[32,2048]{1,0:T(8,128)S(1)} %bitcast.27), kind=kOutput, calls=%fused_computation.19 | convolution fusion | flops 554696704 | bytes 2621440 | tf_op jit(solution)/shard_map/lyg,lxg->lyx/dot_general | solution.py:81
  192.2 0.0 copy-done
  192.3 3.3 convolution_convert_fusion.2
  195.6 0.0 all-gather.8.cloned.1.call-update
  195.6 0.2 reduce-scatter.5.cloned.1.call-start
  195.8 82.0 %all-gather.8.cloned.1.call-done = bf16[1024,4096]{1,0:T(8,128)(2,1)} async-done(((bf16[1024,512]{1,0:T(8,128)(2,1)}), bf16[1024,4096]{1,0:T(8,128)(2,1)}) %all-gather.8.cloned.1.call-update) | async-done | bytes 8388624 | tf_op jit(solution)/shard_map/all_gather | solution.py:99
  277.8 10.2 %convolution_convert_fusion.1 = bf16[4096,512]{1,0:T(8,128)(2,1)} fusion(bf16[1024,4096]{1,0:T(8,128)(2,1)} %all-gather.8.cloned.1.call-done, bf16[1024,512]{1,0:T(8,128)(2,1)} %convolution_convert_fusion.2), kind=kOutput, calls=%fused_computation.9 | convolution fusion | flops 4297064448 | bytes 13631488 | tf_op jit(solution)/shard_map/dot_general | solution.py:100
  288.0 0.0 reduce-scatter.5.cloned.1.call-update
  288.0 0.0 all-gather.10.cloned.1.call-start
  288.0 51.2 %reduce-scatter.5.cloned.1.call-done = bf16[1024,512]{1,0:T(8,128)(2,1)} async-done(((bf16[4096,512]{1,0:T(8,128)(2,1)}), bf16[1024,512]{1,0:T(8,128)(2,1)}) %reduce-scatter.5.cloned.1.call-update) | async-done | bytes 1048592 | tf_op jit(solution)/shard_map/reduce_scatter | solution.py:104
  339.2 0.0 all-gather.10.cloned.1.call-update
  339.3 0.0 all-gather.12.cloned.1.call-start
  339.3 2.4 multiply_reduce_fusion
  341.7 40.4 %psum.23 = f32[]{:T(128)} all-reduce(f32[]{:T(128)} %multiply_reduce_fusion), channel_id=1, replica_groups=mesh['dp'=8,'rot'=4] {'dp','rot'}, use_global_device_ids=true, to_apply=%region_6.7 | all-reduce | flops 1 | bytes 8 | tf_op jit(solution)/shard_map/psum | solution.py:113
  382.8 11.5 %all-gather.10.cloned.1.call-done = bf16[4096,512]{1,0:T(8,128)(2,1)} async-done(((bf16[1024,512]{1,0:T(8,128)(2,1)}), bf16[4096,512]{1,0:T(8,128)(2,1)}) %all-gather.10.cloned.1.call-update) | async-done | bytes 4194320 | tf_op jit(solution)/shard_map/all_gather | solution.py:92
  394.3 10.1 %multiply_convert_fusion.1 = bf16[1024,512]{1,0:T(8,128)(2,1)} fusion(bf16[1024,512]{1,0:T(8,128)(2,1)S(1)} %copy-done.4, bf16[1024,4096]{1,0:T(8,128)(2,1)} %all-gather.8.cloned.1.call-done, bf16[4096,512]{1,0:T(8,128)(2,1)} %all-gather.10.cloned.1.call-done, f32[]{:T(128)S(6)} %mul.79, f32[]{:T(128)S(6)} %div.24), kind=kOutput, calls=%fused_computation.28 | convolution fusion | flops 4298113024 | bytes 14680072 | tf_op jit(solution)/shard_map/dot_general | solution.py:90
  404.4 0.0 all-gather.12.cloned.1.call-update
  404.4 0.3 all-gather.16.cloned.1.call-start
  404.7 81.9 %all-gather.12.cloned.1.call-done = bf16[1024,4096]{1,0:T(8,128)(2,1)} async-done(((bf16[1024,512]{1,0:T(8,128)(2,1)}), bf16[1024,4096]{1,0:T(8,128)(2,1)}) %all-gather.12.cloned.1.call-update) | async-done | bytes 8388624 | tf_op jit(solution)/shard_map/all_gather | solution.py:99
  486.6 10.2 %convolution_convert_fusion = bf16[4096,512]{1,0:T(8,128)(2,1)} fusion(bf16[1024,4096]{1,0:T(8,128)(2,1)} %all-gather.12.cloned.1.call-done, bf16[1024,512]{1,0:T(8,128)(2,1)} %multiply_convert_fusion.1), kind=kOutput, calls=%fused_computation.8 | convolution fusion | flops 4297064448 | bytes 13631488 | tf_op jit(solution)/shard_map/dot_general | solution.py:100
  496.8 0.0 all-gather.16.cloned.1.call-update
  496.8 155.9 %all-gather.16.cloned.1.call-done = bf16[16384,512]{1,0:T(8,128)(2,1)} async-done(((bf16[4096,512]{1,0:T(8,128)(2,1)}), bf16[16384,512]{1,0:T(8,128)(2,1)}) %all-gather.16.cloned.1.call-update) | async-done | bytes 16777232 | tf_op jit(solution)/shard_map/all_gather | solution.py:108
  652.8 11.8 %reduce_sum.32 = bf16[4096,512]{1,0:T(8,128)(2,1)} reduce(bf16[4,4096,512]{2,1,0:T(8,128)(2,1)} %bitcast.24, bf16[]{:T(256)} %constant.75.clone.1), dimensions={0}, to_apply=%region_7.8 | reduce | flops 6291456 | bytes 20971522 | tf_op jit(solution)/shard_map/reduce_sum | solution.py:108
  664.6 10.1 %multiply_convert_fusion = bf16[1024,512]{1,0:T(8,128)(2,1)} fusion(bf16[1024,512]{1,0:T(8,128)(2,1)S(1)} %copy-done.5, bf16[1024,4096]{1,0:T(8,128)(2,1)} %all-gather.12.cloned.1.call-done, bf16[4096,512]{1,0:T(8,128)(2,1)} %reduce_sum.32), kind=kOutput, calls=%fused_computation.27 | convolution fusion | flops 4298113024 | bytes 14680064 | tf_op jit(solution)/shard_map/dot_general | solution.py:120
  (11 shorter events, 0.0 us)
Async XLA Ops:
  7.2 64.0 %reduce-scatter.3.cloned.1.call-start = ((), (), s32[]{:S(2)}) async-start(), calls=%async_computation.2 | async-start | bytes 5242880 | tf_op jit(solution)/shard_map/reduce_scatter | solution.py:55
  15.1 1.0 copy-start.6
  15.1 1.3 copy-start.7
  15.1 131.4 %all-reduce.3.cloned.1.call-start = ((), (), s32[]{:S(2)}) async-start(), calls=%async_computation.9 | async-start | bytes 2228224 | tf_op jit(solution)/shard_map/psum | solution.py:69
  27.5 17.8 %collective-permute-start = (bf16[256,1088]{0,1:T(8,128)(2,1)S(1)}, bf16[256,1088]{0,1:T(8,128)(2,1)S(1)}, u32[]{:S(2)}, u32[]{:S(2)}) collective-permute-start(bf16[256,1088]{0,1:T(8,128)(2,1)S(1)} %get-tuple-element.10), channel_id=1, source_target_pairs={{0,8},{4,12},{8,16},{12,20},{16,24},{20,28},{24,0},{28,4},{1,9},{5... | collective-permute-start | bytes 1671176 | tf_op jit(solution)/shard_map/ppermute | solution.py:45
  29.3 35.9 %collective-permute-start.1 = (bf16[256,1088]{0,1:T(8,128)(2,1)S(1)}, bf16[256,1088]{0,1:T(8,128)(2,1)S(1)}, u32[]{:S(2)}, u32[]{:S(2)}) collective-permute-start(bf16[256,1088]{0,1:T(8,128)(2,1)S(1)} %get-tuple-element.11), channel_id=1, source_target_pairs={{0,16},{4,20},{8,24},{12,28},{16,0},{20,4},{24,8},{28,12},{1,17},{... | collective-permute-start | bytes 1671176 | tf_op jit(solution)/shard_map/ppermute | solution.py:45
  32.3 33.0 %collective-permute-start.2 = (bf16[256,1088]{0,1:T(8,128)(2,1)S(1)}, bf16[256,1088]{0,1:T(8,128)(2,1)S(1)}, u32[]{:S(2)}, u32[]{:S(2)}) collective-permute-start(bf16[256,1088]{0,1:T(8,128)(2,1)S(1)} %get-tuple-element.12), channel_id=1, source_target_pairs={{0,24},{4,28},{8,0},{12,4},{16,8},{20,12},{24,16},{28,20},{1,25},{... | collective-permute-start | bytes 1671176 | tf_op jit(solution)/shard_map/ppermute | solution.py:45
  65.2 0.8 copy-start.1
  65.2 1.0 copy-start.2
  77.6 97.6 %all-gather.14.cloned.1.call-start = ((), (), s32[]{:S(2)}) async-start(), calls=%async_computation.7 | async-start | bytes 1310720 | tf_op jit(solution)/shard_map/all_gather | solution.py:76
  81.9 67.9 %collective-permute-start.3 = (bf16[1024,1056]{0,1:T(8,128)(2,1)}, bf16[1024,1056]{0,1:T(8,128)(2,1)}, u32[]{:S(2)}, u32[]{:S(2)}) collective-permute-start(bf16[1024,1056]{0,1:T(8,128)(2,1)} %fusion.17), channel_id=1, source_target_pairs={{0,4},{4,0},{8,12},{12,8},{16,20},{20,16},{24,28},{28,24},{1,5},{5... | collective-permute-start | bytes 6488072 | tf_op jit(solution)/shard_map/ppermute | solution.py:52
  148.7 2.0 copy-start.3
  149.5 128.3 %all-gather.8.cloned.1.call-start = ((), (), s32[]{:S(2)}) async-start(), calls=%async_computation.3 | async-start | bytes 9437184 | tf_op jit(solution)/shard_map/all_gather | solution.py:99
  176.1 16.1 %copy-start = (bf16[2048,1024]{0,1:T(8,128)(2,1)S(1)}, bf16[2048,1024]{0,1:T(8,128)(2,1)}, u32[]{:S(2)}) copy-start(bf16[2048,1024]{0,1:T(8,128)(2,1)} %fusion.10) | copy-start | bytes 12582916
  195.6 143.6 %reduce-scatter.5.cloned.1.call-start = ((), (), s32[]{:S(2)}) async-start(), calls=%async_computation.4 | async-start | bytes 5242880 | tf_op jit(solution)/shard_map/reduce_scatter | solution.py:104
  288.0 106.4 %copy-start.4 = (bf16[1024,512]{1,0:T(8,128)(2,1)S(1)}, bf16[1024,512]{1,0:T(8,128)(2,1)}, u32[]{:S(2)}) copy-start(bf16[1024,512]{1,0:T(8,128)(2,1)} %convolution_convert_fusion.2) | copy-start | bytes 3145732
  288.0 106.3 %all-gather.10.cloned.1.call-start = ((), (), s32[]{:S(2)}) async-start(), calls=%async_computation.5 | async-start | bytes 5242880 | tf_op jit(solution)/shard_map/all_gather | solution.py:92
  339.3 147.4 %all-gather.12.cloned.1.call-start = ((), (), s32[]{:S(2)}) async-start(), calls=%async_computation.6 | async-start | bytes 9437184 | tf_op jit(solution)/shard_map/all_gather | solution.py:99
  404.4 248.3 %all-gather.16.cloned.1.call-start = ((), (), s32[]{:S(2)}) async-start(), calls=%async_computation.8 | async-start | bytes 20971520 | tf_op jit(solution)/shard_map/all_gather | solution.py:108
  652.8 11.8 %copy-start.5 = (bf16[1024,512]{1,0:T(8,128)(2,1)S(1)}, bf16[1024,512]{1,0:T(8,128)(2,1)}, u32[]{:S(2)}) copy-start(bf16[1024,512]{1,0:T(8,128)(2,1)} %multiply_convert_fusion.1) | copy-start | bytes 3145732
Sparse Core Ops, SparseCore 0:
  15.2 55.9 reduce-scatter.2
  77.7 68.7 all-reduce.2
  149.6 25.4 all-gather.13
  195.7 82.0 all-gather.7
  288.1 51.0 reduce-scatter.4
  340.9 53.3 all-gather.9
  404.6 82.0 all-gather.11
  496.9 155.7 all-gather.15
